TPU v7x, 32 devices: a whole 2x2x4 slice. The times are simulated.
32 devices in a mesh: space: 4 (over z), dp: 8 (over y, x, core).
Axes of the slice: x: 2, y: 2, z: 4, core: 2. Of those that a mesh axis runs over, the one named last changes fastest.
Arguments:
- features: bfloat16 [8, 12, 128, 320], P('dp', 'space'), may hold values from -6 to 6
- cotangent: bfloat16 [8, 12, 128, 320], P('dp', 'space'), may hold values from -6 to 6
- norm_gain: float32 [320], replicated, may hold values from 0.1 to 1.9
- norm_bias: float32 [320], replicated, may hold values from -0.5 to 0.5
- weight: bfloat16 [2880, 320], P('dp'), may hold values from -0.109375 to 0.109375
- moment_one: float32 [2880, 320], P('dp'), may hold values from -332.55374 to 332.55374
- moment_two: float32 [2880, 320], P('dp'), may hold values from 768 to 6144
- heights: int32 [8], P('dp'), may hold values from 6 to 12, as said below
- widths: int32 [8], P('dp'), may hold values from 64 to 128, as said below
Outputs:
- block_out: bfloat16 [8, 12, 128, 320], P('dp', 'space')
- input_grad: bfloat16 [8, 12, 128, 320], P('dp', 'space')
- weight_grad: float32 [2880, 320], P('dp')
- adam_update: float32 [2880, 320], P('dp')
Inputs may be any that keep to these rules, and one draw needn't show every extreme that they name: Image i occupies canvas rows 0 to heights[i] - 1; some image has all 12 rows. Image i occupies canvas columns 0 to widths[i] - 1; some image has all 128 columns.
All inputs are finite; a program needn't handle non-finite values.
Results may differ from a plain program's by a relative error of at most 0.017.
Values may be sent and summed in bfloat16 or wider, within the bound.
No kernel may reach another device: no remote copies, remote signals or barrier semaphores. Data moves between devices by JAX's collectives and lax.ppermute only.
A program may use at most 64 MiB of HBM per device.

v0:
```python
import jax
import jax.numpy as jnp
from jax import lax
from jax.sharding import PartitionSpec as P

GROUPS = 32


def with_halo(cells, sides, width):
    for axis, dim in sides:
        count = lax.axis_size(axis)
        ends = count - 1
        head = lax.slice_in_dim(cells, 0, width, axis=dim)
        tail = lax.slice_in_dim(cells, cells.shape[dim] - width, cells.shape[dim], axis=dim)
        cells = jnp.concatenate(
            [
                lax.ppermute(tail, axis, [(i, (i + 1) % count) for i in range(ends)]),
                cells,
                lax.ppermute(head, axis, [((i + 1) % count, i) for i in range(ends)]),
            ],
            axis=dim,
        )
    return cells


def space_sum(parts, axis):
    count = lax.axis_size(axis)
    if count & count - 1:
        return lax.psum(parts, axis)
    step = 1
    while step < count:
        pairs = [(i, i ^ step) for i in range(count)]
        parts = tuple((p + q for p, q in zip(parts, lax.ppermute(parts, axis, pairs))))
        step *= 2
    return parts


def group_sum(values, groups):
    height_dev, width_dev, channels = values.shape
    return values.reshape(height_dev, width_dev, groups, channels // groups).sum(axis=(0, 1, 3))


def spread_groups(statistic, channels):
    return jnp.repeat(statistic, channels // statistic.shape[0])


def pad_columns(padded_rows):
    return jnp.pad(padded_rows, ((0, 0), (1, 1), (0, 0)))


def local(
    features, cotangent, norm_gain, norm_bias, weight, moment_one, moment_two, heights, widths
):
    latent = features[0]
    height_dev, width_dev, channels = latent.shape
    row_ids = lax.axis_index("space") * height_dev + jnp.arange(height_dev, dtype=jnp.int32)
    inside = (
        (row_ids < heights[0])[:, None]
        & (jnp.arange(width_dev, dtype=jnp.int32) < widths[0])[None, :]
    ).astype(jnp.float32)[..., None]
    cell_count = (heights[0] * widths[0] * (channels // GROUPS)).astype(jnp.float32)
    gathered = lax.all_gather(weight, "dp", axis=0, tiled=True)
    tap_weights = gathered.reshape(9, channels, channels)
    values = latent.astype(jnp.float32) * inside
    group_total, squares = space_sum(
        (group_sum(values, GROUPS), group_sum(values * values, GROUPS)), "space"
    )
    center = group_total / cell_count
    spread = squares / cell_count - center * center
    inverse = lax.rsqrt(spread + 1e-05)
    normed = (values - spread_groups(center, channels)) * spread_groups(inverse, channels) * inside
    before = normed * norm_gain + norm_bias
    activated = (jax.nn.silu(before) * inside).astype(jnp.bfloat16)
    act_pad = pad_columns(with_halo(activated, (("space", 0),), 1))
    output = jnp.zeros((height_dev * width_dev, channels), jnp.float32)
    for row_off in range(3):
        for col_off in range(3):
            window = act_pad[row_off : row_off + height_dev, col_off : col_off + width_dev].reshape(
                -1, channels
            )
            output = output + jnp.dot(
                window, tap_weights[row_off * 3 + col_off], preferred_element_type=jnp.float32
            )
    block_out = (output.reshape(height_dev, width_dev, channels) * inside).astype(jnp.bfloat16)
    masked = cotangent[0] * inside.astype(jnp.bfloat16)
    cot_pad = pad_columns(with_halo(masked, (("space", 0),), 1))
    flat_cot = masked.reshape(-1, channels)
    upstream = jnp.zeros((height_dev * width_dev, channels), jnp.float32)
    tap_grads = []
    for row_off in range(3):
        for col_off in range(3):
            tap_index = row_off * 3 + col_off
            window = act_pad[row_off : row_off + height_dev, col_off : col_off + width_dev].reshape(
                -1, channels
            )
            tap_grads.append(
                lax.dot_general(
                    window, flat_cot, (((0,), (0,)), ((), ())), preferred_element_type=jnp.float32
                )
            )
            cot_window = cot_pad[
                2 - row_off : 2 - row_off + height_dev, 2 - col_off : 2 - col_off + width_dev
            ].reshape(-1, channels)
            upstream = upstream + lax.dot_general(
                cot_window,
                tap_weights[tap_index],
                (((1,), (1,)), ((), ())),
                preferred_element_type=jnp.float32,
            )
    weight_terms = jnp.stack(tap_grads).reshape(9 * channels, channels)
    gate_sig = jax.nn.sigmoid(before)
    silu_slope = gate_sig * (1.0 + before * (1.0 - gate_sig))
    scaled = upstream.reshape(height_dev, width_dev, channels) * silu_slope * inside * norm_gain
    local_first = group_sum(scaled, GROUPS)
    local_second = group_sum(scaled * normed, GROUPS)
    dp_size = lax.axis_size("dp")
    grad_piece = lax.psum_scatter(
        weight_terms.astype(jnp.bfloat16).reshape(dp_size, -1, channels),
        "dp",
        scatter_dimension=0,
        tiled=False,
    )
    sum_first, sum_second = space_sum((local_first, local_second), "space")
    grad_piece = lax.psum(grad_piece, "space").astype(jnp.float32)
    first = sum_first / cell_count
    second = sum_second / cell_count
    input_grad = (
        spread_groups(inverse, channels)
        * (scaled - spread_groups(first, channels) - normed * spread_groups(second, channels))
        * inside
    ).astype(jnp.bfloat16)
    first_new = 0.9 * moment_one + 0.1 * grad_piece
    second_new = 0.999 * moment_two + 0.001 * grad_piece * grad_piece
    adam_update = first_new / (1.0 - 0.9**10) / (jnp.sqrt(second_new / (1.0 - 0.999**10)) + 1e-08)
    return (block_out[None], input_grad[None], grad_piece, adam_update)


def solution(mesh):
    placed = (
        P("dp", "space", None, None),
        P("dp", "space", None, None),
        P(),
        P(),
        P("dp", None),
        P("dp", None),
        P("dp", None),
        P("dp"),
        P("dp"),
    )
    return jax.shard_map(
        local,
        mesh=mesh,
        in_specs=placed,
        out_specs=(
            P("dp", "space", None, None),
            P("dp", "space", None, None),
            P("dp", None),
            P("dp", None),
        ),
        check_vma=False,
    )
```

profile of v0, /device:TPU:0, one launch (start us, length us, event | category | flops | bytes accessed | tf_op | source)
XLA Modules:
  0.0 191.6 jit_solution(13779045567825138440)
XLA Ops:
  8.6 1.1 multiply_reduce_fusion.1
  10.0 3.1 %collective-permute-start = (f32[32]{0:T(128)S(1)}, f32[32]{0:T(128)S(1)}, u32[]{:S(2)}, u32[]{:S(2)}) collective-permute-start(f32[32]{0:T(128)S(1)} %reduce_sum.51), channel_id=1, source_target_pairs={{0,8},{8,0},{16,24},{24,16},{1,9},{9,1},{17,25},{25,17},{2,10},{10... | collective-permute-start | bytes 392 | tf_op jit(solution)/shard_map/ppermute | solution.py:33
  13.4 1.2 collective-permute-done
  14.6 3.0 %collective-permute-start.1 = (f32[32]{0:T(128)S(1)}, f32[32]{0:T(128)S(1)}, u32[]{:S(2)}, u32[]{:S(2)}) collective-permute-start(f32[32]{0:T(128)S(1)} %add.163), channel_id=1, source_target_pairs={{0,16},{8,24},{16,0},{24,8},{1,17},{9,25},{17,1},{25,9},{2,18},{10... | collective-permute-start | bytes 392 | tf_op jit(solution)/shard_map/ppermute | solution.py:33
  17.6 1.9 collective-permute-start.3
  19.5 2.6 %collective-permute-done.3 = f32[32]{0:T(128)S(1)} collective-permute-done((f32[32]{0:T(128)S(1)}, f32[32]{0:T(128)S(1)}, u32[]{:S(2)}, u32[]{:S(2)}) %collective-permute-start.3) | collective-permute-done | bytes 160 | tf_op jit(solution)/shard_map/ppermute | solution.py:33
  22.5 1.3 multiply_convert_fusion.4
  23.7 3.5 %collective-permute-start.4 = (bf16[1,128,320]{1,2,0:T(8,128)(2,1)S(1)}, bf16[1,128,320]{1,2,0:T(8,128)(2,1)S(1)}, u32[]{:S(2)}, u32[]{:S(2)}) collective-permute-start(bf16[1,128,320]{1,2,0:T(8,128)(2,1)S(1)} %get-tuple-element.30), channel_id=1, source_target_pairs={{0,8},{8,16},{16,24},{1,9},{9,17},{17,25},{2,10},{10,18},{18,26},{... | collective-permute-start | bytes 245768 | tf_op jit(solution)/shard_map/ppermute | solution.py:17
  27.2 1.3 collective-permute-start.5
  28.5 1.0 bitcast_multiply_fusion.2
  29.5 4.1 %collective-permute-done.5 = bf16[1,128,320]{1,2,0:T(8,128)(2,1)S(1)} collective-permute-done((bf16[1,128,320]{1,2,0:T(8,128)(2,1)S(1)}, bf16[1,128,320]{1,2,0:T(8,128)(2,1)S(1)}, u32[]{:S(2)}, u32[]{:S(2)}) %collective-permute-start.5) | collective-permute-done | bytes 81952 | tf_op jit(solution)/shard_map/ppermute | solution.py:19
  34.0 1.0 fusion.29
  35.0 1.0 fusion.15
  36.0 1.1 fusion.27
  37.1 1.0 fusion.25
  38.1 1.2 fusion.23
  39.4 1.1 fusion.21
  40.4 1.0 fusion.19
  41.4 1.1 fusion.13
  42.5 1.1 fusion.17
  43.6 4.2 %copy.68 = bf16[8,360,320]{1,2,0:T(8,128)(2,1)} copy(bf16[8,360,320]{2,1,0:T(8,128)(2,1)} %bitcast.48) | data formatting | bytes 3686400 | tf_op jit(solution)/shard_map/convert_element_type | solution.py:118
  47.8 38.9 %reduce-scatter.2.cloned.1.call-done = bf16[1,360,320]{1,2,0:T(8,128)(2,1)} async-done(((bf16[8,360,320]{1,2,0:T(8,128)(2,1)}), bf16[1,360,320]{1,2,0:T(8,128)(2,1)}) %reduce-scatter.2.cloned.1.call-update) | async-done | bytes 230416 | tf_op jit(solution)/shard_map/reduce_scatter | solution.py:117
  87.5 3.4 %collective-permute-start.6 = (bf16[1,128,320]{1,2,0:T(8,128)(2,1)S(1)}, bf16[1,128,320]{1,2,0:T(8,128)(2,1)S(1)}, u32[]{:S(2)}, u32[]{:S(2)}) collective-permute-start(bf16[1,128,320]{1,2,0:T(8,128)(2,1)S(1)} %get-tuple-element.26), channel_id=1, source_target_pairs={{0,8},{8,16},{16,24},{1,9},{9,17},{17,25},{2,10},{10,18},{18,26},{... | collective-permute-start | bytes 245768 | tf_op jit(solution)/shard_map/ppermute | solution.py:17
  90.9 1.3 collective-permute-start.7
  92.8 1.0 copy.49
  93.8 4.8 %collective-permute-done.7 = bf16[1,128,320]{1,2,0:T(8,128)(2,1)S(1)} collective-permute-done((bf16[1,128,320]{1,2,0:T(8,128)(2,1)S(1)}, bf16[1,128,320]{1,2,0:T(8,128)(2,1)S(1)}, u32[]{:S(2)}, u32[]{:S(2)}) %collective-permute-start.7) | collective-permute-done | bytes 81952 | tf_op jit(solution)/shard_map/ppermute | solution.py:19
  100.9 1.7 pad_maximum_fusion
  102.6 1.8 copy.57
  105.3 0.9 copy.59
  109.0 0.9 copy.64
  109.9 1.0 fusion.102
  110.9 1.2 copy.43
  112.1 0.9 copy.45
  115.7 0.9 copy.50
  117.1 7.1 %all-reduce.4.cloned.1.call-done = bf16[360,320]{0,1:T(8,128)(2,1)} async-done(((bf16[360,320]{0,1:T(8,128)(2,1)}), bf16[360,320]{0,1:T(8,128)(2,1)}) %all-reduce.4.cloned.1.call-update) | async-done | bytes 230416 | tf_op jit(solution)/shard_map/psum | solution.py:124
  124.2 2.3 %fusion.35 = (f32[360,320]{0,1:T(8,128)}, f32[360,320]{0,1:T(8,128)}) fusion(f32[360,320]{0,1:T(8,128)S(1)} %copy-done.11, f32[360,320]{0,1:T(8,128)} %param.14, bf16[360,320]{0,1:T(8,128)(2,1)} %all-reduce.4.cloned.1.call-done), kind=kLoop, calls=%fused_computation.65 | loop fusion | flops 1382400 | bytes 2073600 | tf_op jit(solution)/shard_map/div | solution.py:134
  126.5 27.0 %all-gather.3.cloned.1.call-done = bf16[8,360,320]{1,2,0:T(8,128)(2,1)} async-done(((bf16[1,360,320]{1,2,0:T(8,128)(2,1)}), bf16[8,360,320]{1,2,0:T(8,128)(2,1)}) %all-gather.3.cloned.1.call-update) | async-done | bytes 1843216 | tf_op jit(solution)/shard_map/all_gather | solution.py:62
  153.5 4.0 %copy.44 = bf16[8,360,320]{1,0,2:T(8,128)(2,1)} copy(bf16[8,360,320]{1,2,0:T(8,128)(2,1)} %all-gather.3.cloned.1.call-done) | data formatting | bytes 3686400 | tf_op jit(solution)/shard_map/all_gather | solution.py:62
  157.4 3.4 %reshape.284 = bf16[2880,320]{0,1:T(8,128)(2,1)S(1)} reshape(bf16[8,360,320]{1,0,2:T(8,128)(2,1)} %copy.44) | data formatting | bytes 3686400
  161.2 1.3 fusion.68
  166.1 1.4 fusion.81
  167.5 1.5 convolution_add_fusion.8
  173.0 1.6 collective-permute-start.8
  175.6 1.0 collective-permute-done.8
  176.6 2.4 %collective-permute-start.9 = (f32[32]{0:T(128)S(1)}, f32[32]{0:T(128)S(1)}, u32[]{:S(2)}, u32[]{:S(2)}) collective-permute-start(f32[32]{0:T(128)S(1)} %add.198), channel_id=1, source_target_pairs={{0,16},{8,24},{16,0},{24,8},{1,17},{9,25},{17,1},{25,9},{2,18},{10... | collective-permute-start | bytes 392 | tf_op jit(solution)/shard_map/ppermute | solution.py:33
  179.0 1.8 collective-permute-start.11
  181.0 2.4 %collective-permute-done.11 = f32[32]{0:T(128)S(1)} collective-permute-done((f32[32]{0:T(128)S(1)}, f32[32]{0:T(128)S(1)}, u32[]{:S(2)}, u32[]{:S(2)}) %collective-permute-start.11) | collective-permute-done | bytes 160 | tf_op jit(solution)/shard_map/ppermute | solution.py:33
  183.8 1.3 multiply_convert_fusion.1
  (116 shorter events, 21.2 us)
Async XLA Ops:
  7.2 79.6 %reduce-scatter.2.cloned.1.call-start = ((), (), s32[]{:S(2)}) async-start(), calls=%async_computation.1 | async-start | bytes 2211840 | tf_op jit(solution)/shard_map/reduce_scatter | solution.py:117
  10.0 4.6 %collective-permute-start = (f32[32]{0:T(128)S(1)}, f32[32]{0:T(128)S(1)}, u32[]{:S(2)}, u32[]{:S(2)}) collective-permute-start(f32[32]{0:T(128)S(1)} %reduce_sum.51), channel_id=1, source_target_pairs={{0,8},{8,0},{16,24},{24,16},{1,9},{9,1},{17,25},{25,17},{2,10},{10... | collective-permute-start | bytes 392 | tf_op jit(solution)/shard_map/ppermute | solution.py:33
  13.3 4.3 %collective-permute-start.2 = (f32[32]{0:T(128)S(1)}, f32[32]{0:T(128)S(1)}, u32[]{:S(2)}, u32[]{:S(2)}) collective-permute-start(f32[32]{0:T(128)S(1)} %reduce_sum.54), channel_id=1, source_target_pairs={{0,8},{8,0},{16,24},{24,16},{1,9},{9,1},{17,25},{25,17},{2,10},{10... | collective-permute-start | bytes 392 | tf_op jit(solution)/shard_map/ppermute | solution.py:33
  14.6 4.9 %collective-permute-start.1 = (f32[32]{0:T(128)S(1)}, f32[32]{0:T(128)S(1)}, u32[]{:S(2)}, u32[]{:S(2)}) collective-permute-start(f32[32]{0:T(128)S(1)} %add.163), channel_id=1, source_target_pairs={{0,16},{8,24},{16,0},{24,8},{1,17},{9,25},{17,1},{25,9},{2,18},{10... | collective-permute-start | bytes 392 | tf_op jit(solution)/shard_map/ppermute | solution.py:33
  17.6 4.4 %collective-permute-start.3 = (f32[32]{0:T(128)S(1)}, f32[32]{0:T(128)S(1)}, u32[]{:S(2)}, u32[]{:S(2)}) collective-permute-start(f32[32]{0:T(128)S(1)} %add.165), channel_id=1, source_target_pairs={{0,16},{8,24},{16,0},{24,8},{1,17},{9,25},{17,1},{25,9},{2,18},{10... | collective-permute-start | bytes 392 | tf_op jit(solution)/shard_map/ppermute | solution.py:33
  23.7 5.8 %collective-permute-start.4 = (bf16[1,128,320]{1,2,0:T(8,128)(2,1)S(1)}, bf16[1,128,320]{1,2,0:T(8,128)(2,1)S(1)}, u32[]{:S(2)}, u32[]{:S(2)}) collective-permute-start(bf16[1,128,320]{1,2,0:T(8,128)(2,1)S(1)} %get-tuple-element.30), channel_id=1, source_target_pairs={{0,8},{8,16},{16,24},{1,9},{9,17},{17,25},{2,10},{10,18},{18,26},{... | collective-permute-start | bytes 245768 | tf_op jit(solution)/shard_map/ppermute | solution.py:17
  27.2 6.3 %collective-permute-start.5 = (bf16[1,128,320]{1,2,0:T(8,128)(2,1)S(1)}, bf16[1,128,320]{1,2,0:T(8,128)(2,1)S(1)}, u32[]{:S(2)}, u32[]{:S(2)}) collective-permute-start(bf16[1,128,320]{1,2,0:T(8,128)(2,1)S(1)} %get-tuple-element.31), channel_id=1, source_target_pairs={{8,0},{16,8},{24,16},{9,1},{17,9},{25,17},{10,2},{18,10},{26,18},{... | collective-permute-start | bytes 245768 | tf_op jit(solution)/shard_map/ppermute | solution.py:19
  34.0 4.2 %copy-start = (bf16[1,3,128,320]{2,3,1,0:T(8,128)(2,1)S(1)}, bf16[1,3,128,320]{2,3,1,0:T(8,128)(2,1)}, u32[]{:S(2)}) copy-start(bf16[1,3,128,320]{2,3,1,0:T(8,128)(2,1)} %param.9) | copy-start | bytes 737284
  34.0 4.2 %copy-start.10 = (bf16[1,3,128,320]{2,3,1,0:T(8,128)(2,1)S(1)}, bf16[1,3,128,320]{2,3,1,0:T(8,128)(2,1)}, u32[]{:S(2)}) copy-start(bf16[1,3,128,320]{2,3,1,0:T(8,128)(2,1)} %param.10) | copy-start | bytes 737284
  34.0 4.1 %copy-start.17 = (f32[320]{0:T(512)S(1)}, f32[320]{0:T(512)}, u32[]{:S(2)}) copy-start(f32[320]{0:T(512)} %param.12) | copy-start | bytes 3844
  34.0 4.1 %copy-start.18 = (f32[320]{0:T(512)S(1)}, f32[320]{0:T(512)}, u32[]{:S(2)}) copy-start(f32[320]{0:T(512)} %param.11) | copy-start | bytes 3844
  47.8 76.4 %all-reduce.4.cloned.1.call-start = ((), (), s32[]{:S(2)}) async-start(), calls=%async_computation.2 | async-start | bytes 491520 | tf_op jit(solution)/shard_map/psum | solution.py:124
  86.8 66.7 %all-gather.3.cloned.1.call-start = ((), (), s32[]{:S(2)}) async-start(), calls=%async_computation.3 | async-start | bytes 2211840 | tf_op jit(solution)/shard_map/all_gather | solution.py:62
  87.5 6.3 %collective-permute-start.6 = (bf16[1,128,320]{1,2,0:T(8,128)(2,1)S(1)}, bf16[1,128,320]{1,2,0:T(8,128)(2,1)S(1)}, u32[]{:S(2)}, u32[]{:S(2)}) collective-permute-start(bf16[1,128,320]{1,2,0:T(8,128)(2,1)S(1)} %get-tuple-element.26), channel_id=1, source_target_pairs={{0,8},{8,16},{16,24},{1,9},{9,17},{17,25},{2,10},{10,18},{18,26},{... | collective-permute-start | bytes 245768 | tf_op jit(solution)/shard_map/ppermute | solution.py:17
  90.9 7.7 %collective-permute-start.7 = (bf16[1,128,320]{1,2,0:T(8,128)(2,1)S(1)}, bf16[1,128,320]{1,2,0:T(8,128)(2,1)S(1)}, u32[]{:S(2)}, u32[]{:S(2)}) collective-permute-start(bf16[1,128,320]{1,2,0:T(8,128)(2,1)S(1)} %get-tuple-element.27), channel_id=1, source_target_pairs={{8,0},{16,8},{24,16},{9,1},{17,9},{25,17},{10,2},{18,10},{26,18},{... | collective-permute-start | bytes 245768 | tf_op jit(solution)/shard_map/ppermute | solution.py:19
  93.8 4.8 %copy-start.14 = (bf16[1,128,320]{1,2,0:T(8,128)(2,1)}, bf16[1,128,320]{1,2,0:T(8,128)(2,1)S(1)}, u32[]{:S(2)}) copy-start(bf16[1,128,320]{1,2,0:T(8,128)(2,1)S(1)} %collective-permute-done.6) | copy-start | bytes 245764
  98.7 0.6 copy-start.15
  113.0 11.2 %copy-start.11 = (f32[360,320]{0,1:T(8,128)S(1)}, f32[360,320]{0,1:T(8,128)}, u32[]{:S(2)}) copy-start(f32[360,320]{0,1:T(8,128)} %param.15) | copy-start | bytes 1382404
  160.8 1.7 copy-start.9
  160.8 2.1 %copy-start.8 = (bf16[3,128,320]{2,1,0:T(8,128)(2,1)S(1)}, bf16[3,128,320]{2,1,0:T(8,128)(2,1)}, u32[]{:S(2)}) copy-start(bf16[3,128,320]{2,1,0:T(8,128)(2,1)} %copy.45) | copy-start | bytes 737284
  161.2 2.1 %copy-start.7 = (bf16[3,128,320]{2,1,0:T(8,128)(2,1)S(1)}, bf16[3,128,320]{2,1,0:T(8,128)(2,1)}, u32[]{:S(2)}) copy-start(bf16[3,128,320]{2,1,0:T(8,128)(2,1)} %copy.46) | copy-start | bytes 737284
  162.5 1.1 copy-start.6
  163.3 1.1 copy-start.12
  166.1 2.9 %copy-start.5 = (bf16[3,128,320]{2,1,0:T(8,128)(2,1)S(1)}, bf16[3,128,320]{2,1,0:T(8,128)(2,1)}, u32[]{:S(2)}) copy-start(bf16[3,128,320]{2,1,0:T(8,128)(2,1)} %copy.58) | copy-start | bytes 737284
  166.1 3.3 %copy-start.4 = (bf16[3,128,320]{2,1,0:T(8,128)(2,1)S(1)}, bf16[3,128,320]{2,1,0:T(8,128)(2,1)}, u32[]{:S(2)}) copy-start(bf16[3,128,320]{2,1,0:T(8,128)(2,1)} %copy.59) | copy-start | bytes 737284
  169.4 1.0 copy-start.3
  169.9 1.0 copy-start.1
  170.3 1.0 copy-start.2
  170.9 1.1 copy-start.13
  170.9 1.1 copy-start.16
  173.0 3.6 %collective-permute-start.8 = (f32[32]{0:T(128)S(1)}, f32[32]{0:T(128)S(1)}, u32[]{:S(2)}, u32[]{:S(2)}) collective-permute-start(f32[32]{0:T(128)S(1)} %reduce_sum.72), channel_id=1, source_target_pairs={{0,8},{8,0},{16,24},{24,16},{1,9},{9,1},{17,25},{25,17},{2,10},{10... | collective-permute-start | bytes 392 | tf_op jit(solution)/shard_map/ppermute | solution.py:33
  174.7 4.3 %collective-permute-start.10 = (f32[32]{0:T(128)S(1)}, f32[32]{0:T(128)S(1)}, u32[]{:S(2)}, u32[]{:S(2)}) collective-permute-start(f32[32]{0:T(128)S(1)} %reduce_sum.75), channel_id=1, source_target_pairs={{0,8},{8,0},{16,24},{24,16},{1,9},{9,1},{17,25},{25,17},{2,10},{10... | collective-permute-start | bytes 392 | tf_op jit(solution)/shard_map/ppermute | solution.py:33
  176.6 4.4 %collective-permute-start.9 = (f32[32]{0:T(128)S(1)}, f32[32]{0:T(128)S(1)}, u32[]{:S(2)}, u32[]{:S(2)}) collective-permute-start(f32[32]{0:T(128)S(1)} %add.198), channel_id=1, source_target_pairs={{0,16},{8,24},{16,0},{24,8},{1,17},{9,25},{17,1},{25,9},{2,18},{10... | collective-permute-start | bytes 392 | tf_op jit(solution)/shard_map/ppermute | solution.py:33
  179.0 4.4 %collective-permute-start.11 = (f32[32]{0:T(128)S(1)}, f32[32]{0:T(128)S(1)}, u32[]{:S(2)}, u32[]{:S(2)}) collective-permute-start(f32[32]{0:T(128)S(1)} %add.200), channel_id=1, source_target_pairs={{0,16},{8,24},{16,0},{24,8},{1,17},{9,25},{17,1},{25,9},{2,18},{10... | collective-permute-start | bytes 392 | tf_op jit(solution)/shard_map/ppermute | solution.py:33
Sparse Core Ops, SparseCore 0:
  47.9 38.8 reduce-scatter.1
  89.2 34.9 all-reduce.3
  126.1 27.3 all-gather.2
where the time goes:
time: 192 us
  waiting for transfers between devices  89.9 us (47%)
  local copies, waits for them, and re-layouts  31.8 us (17%)
  starting transfers between devices  24 us (12%)
  matrix products  20.2 us (11%)
  between operations  15.6 us (8%)
  other arithmetic  10.2 us (5%)
    reduce_scatter x1, waiting for transfers between devices, local(): lax.psum_scatter(weight_terms.astype(jnp.bfloat16).reshape(dp_size, -1, c...  38.9 us
    all_gather x1, waiting for transfers between devices, local(): gathered = lax.all_gather(weight, 'dp', axis=0, tiled=True)  27 us
    ppermute x8, starting transfers between devices, space_sum(): lax.ppermute(parts, axis, pairs)  14.4 us
    dot_general x9, matrix products, local(): lax.dot_general(window, flat_cot, (((0,), (0,)), ((), ())), preferred_ele...  9.52 us
    ppermute x2, waiting for transfers between devices, with_halo(): lax.ppermute(head, axis, [((i + 1) % count, i) for i in range(ends)])  8.87 us
    slice x9, local copies, waits for them, and re-layouts, local(): cot_pad[2 - row_off:2 - row_off + height_dev, 2 - col_off:2 - col_off + w...  8.5 us
    ppermute x8, waiting for transfers between devices, space_sum(): lax.ppermute(parts, axis, pairs)  7.28 us
    slice x9, local copies, waits for them, and re-layouts, local(): act_pad[row_off:row_off + height_dev, col_off:col_off + width_dev]  7.13 us
  transfers between devices with their start and end apart: 15, of which 9 were waited for; matrix products, arithmetic and copies ran while one was open for 12% of the time, Pallas kernels for 0%

commit v1 on v0

--- a/solution.py
+++ b/solution.py
@@ -59,7 +59,16 @@
         & (jnp.arange(width_dev, dtype=jnp.int32) < widths[0])[None, :]
     ).astype(jnp.float32)[..., None]
     cell_count = (heights[0] * widths[0] * (channels // GROUPS)).astype(jnp.float32)
-    gathered = lax.all_gather(weight, "dp", axis=0, tiled=True)
+    ways = lax.axis_size("dp")
+    up = [(d, (d + 1) % ways) for d in range(ways)]
+    down = [(d, (d - 1) % ways) for d in range(ways)]
+    earlier, later = ([weight], [weight])
+    for _ in range(ways // 2):
+        earlier.append(lax.ppermute(earlier[-1], "dp", up))
+    for _ in range((ways - 1) // 2):
+        later.append(lax.ppermute(later[-1], "dp", down))
+    line = jnp.concatenate([*earlier[::-1], *later[1:]], axis=0)
+    gathered = jnp.roll(line, (lax.axis_index("dp") - ways // 2) * weight.shape[0], axis=0)
     tap_weights = gathered.reshape(9, channels, channels)
     values = latent.astype(jnp.float32) * inside
     group_total, squares = space_sum(

time: 192 us -> 168 us (0.88)
  waiting for transfers between devices: 89.9 us -> 51 us
  matrix products: 20.2 us -> 30.2 us
  starting transfers between devices: 24 us -> 32 us
  local copies, waits for them, and re-layouts: 31.8 us -> 27.6 us
    reduce_scatter x1, waiting for transfers between devices: 38.9 us -> 0.02 us  [local(): lax.psum_scatter(weight_terms.astype(jnp.bfloat16).reshape(dp_size, -1, c...]
    all_gather x1 -> x0, waiting for transfers between devices: 27 us -> none  [local(): gathered = lax.all_gather(weight, 'dp', axis=0, tiled=True)]
    psum x1, waiting for transfers between devices: 7.13 us -> 34.1 us  [local(): grad_piece = lax.psum(grad_piece, 'space').astype(jnp.float32)]
    ppermute x0 -> x7, waiting for transfers between devices: none -> 10.6 us  [the longest x4 10.6 us: local(): earlier.append(lax.ppermute(earlier[-1], 'dp', up))]
    ppermute x0 -> x7, starting transfers between devices: none -> 8.88 us  [the longest x3 8.32 us: local(): later.append(lax.ppermute(later[-1], 'dp', down))]
    ppermute x2, waiting for transfers between devices: 8.87 us -> 0.01 us  [with_halo(): lax.ppermute(head, axis, [((i + 1) % count, i) for i in range(ends)])]
    dot_general x9, matrix products: 4.33 us -> 12.5 us  [local(): jnp.dot(window, tap_weights[row_off * 3 + col_off], preferred_element_typ...]
    dot_general x9, matrix products: 6.32 us -> 14.4 us  [local(): lax.dot_general(cot_window, tap_weights[tap_index], (((1,), (1,)), ((), (...]
  transfers between devices with their start and end apart: 15 -> 21, of which waited for: 9 -> 8; matrix products, arithmetic and copies ran while one was open for 12% -> 38% of each run, Pallas kernels for 0% -> 0%
where the time goes in v1:
time: 168 us; the launch traced here: 166 us
  waiting for transfers between devices  51 us (30%)
  starting transfers between devices  32 us (19%)
  matrix products  30.2 us (18%)
  local copies, waits for them, and re-layouts  27.6 us (16%)
  between operations  16.2 us (10%)
  other arithmetic  8.81 us (5%)
    psum x1, waiting for transfers between devices, local(): grad_piece = lax.psum(grad_piece, 'space').astype(jnp.float32)  34.1 us
    dot_general x9, matrix products, local(): lax.dot_general(cot_window, tap_weights[tap_index], (((1,), (1,)), ((), (...  14.4 us
    ppermute x8, starting transfers between devices, space_sum(): lax.ppermute(parts, axis, pairs)  13.1 us
    dot_general x9, matrix products, local(): jnp.dot(window, tap_weights[row_off * 3 + col_off], preferred_element_typ...  12.5 us
    ppermute x4, waiting for transfers between devices, local(): earlier.append(lax.ppermute(earlier[-1], 'dp', up))  10.6 us
    ppermute x3, starting transfers between devices, local(): later.append(lax.ppermute(later[-1], 'dp', down))  8.32 us
    concatenate x1, local copies, waits for them, and re-layouts, local(): jnp.roll(line, (lax.axis_index('dp') - ways // 2) * weight.shape[0], axis=0)  7.53 us
    slice x9, local copies, waits for them, and re-layouts, local(): cot_pad[2 - row_off:2 - row_off + height_dev, 2 - col_off:2 - col_off + w...  7.5 us
  transfers between devices with their start and end apart: 21, of which 8 were waited for; matrix products, arithmetic and copies ran while one was open for 38% of the time, Pallas kernels for 0%

profile of v1, /device:TPU:0, one launch (start us, length us, event | category | flops | bytes accessed | tf_op | source)
XLA Modules:
  0.0 165.9 jit_solution(2621591263001036346)
XLA Ops:
  7.8 2.9 %collective-permute-start.10 = (bf16[360,320]{0,1:T(8,128)(2,1)}, bf16[360,320]{0,1:T(8,128)(2,1)}, u32[]{:S(2)}, u32[]{:S(2)}) collective-permute-start(bf16[360,320]{0,1:T(8,128)(2,1)} %param.13), channel_id=1, source_target_pairs={{0,7},{1,0},{2,1},{3,2},{4,3},{5,4},{6,5},{7,6},{8,15},{9,8},{10,9... | collective-permute-start | bytes 691208 | tf_op jit(solution)/shard_map/ppermute | solution.py:69
  12.1 1.1 multiply_reduce_fusion.1
  13.5 2.3 %collective-permute-start = (f32[32]{0:T(128)S(1)}, f32[32]{0:T(128)S(1)}, u32[]{:S(2)}, u32[]{:S(2)}) collective-permute-start(f32[32]{0:T(128)S(1)} %reduce_sum.51), channel_id=1, source_target_pairs={{0,8},{8,0},{16,24},{24,16},{1,9},{9,1},{17,25},{25,17},{2,10},{10... | collective-permute-start | bytes 392 | tf_op jit(solution)/shard_map/ppermute | solution.py:33
  16.1 1.0 bitcast_multiply_fusion.2
  17.1 3.9 %collective-permute-start.13 = (bf16[1,128,320]{1,2,0:T(8,128)(2,1)S(1)}, bf16[1,128,320]{1,2,0:T(8,128)(2,1)S(1)}, u32[]{:S(2)}, u32[]{:S(2)}) collective-permute-start(bf16[1,128,320]{1,2,0:T(8,128)(2,1)S(1)} %get-tuple-element.26), channel_id=1, source_target_pairs={{0,8},{8,16},{16,24},{1,9},{9,17},{17,25},{2,10},{10,18},{18,26},{... | collective-permute-start | bytes 245768 | tf_op jit(solution)/shard_map/ppermute | solution.py:17
  21.7 1.1 copy.21
  22.8 1.2 copy.33
  25.1 2.7 %collective-permute-start.1 = (f32[32]{0:T(128)S(1)}, f32[32]{0:T(128)S(1)}, u32[]{:S(2)}, u32[]{:S(2)}) collective-permute-start(f32[32]{0:T(128)S(1)} %add.174), channel_id=1, source_target_pairs={{0,16},{8,24},{16,0},{24,8},{1,17},{9,25},{17,1},{25,9},{2,18},{10... | collective-permute-start | bytes 392 | tf_op jit(solution)/shard_map/ppermute | solution.py:33
  28.1 1.5 collective-permute-done.1
  29.6 1.3 collective-permute-start.14
  30.9 1.3 collective-permute-done.3
  32.9 3.3 %collective-permute-start.4 = (bf16[1,128,320]{1,2,0:T(8,128)(2,1)S(1)}, bf16[1,128,320]{1,2,0:T(8,128)(2,1)S(1)}, u32[]{:S(2)}, u32[]{:S(2)}) collective-permute-start(bf16[1,128,320]{1,2,0:T(8,128)(2,1)S(1)} %get-tuple-element.30), channel_id=1, source_target_pairs={{0,8},{8,16},{16,24},{1,9},{9,17},{17,25},{2,10},{10,18},{18,26},{... | collective-permute-start | bytes 245768 | tf_op jit(solution)/shard_map/ppermute | solution.py:17
  36.2 1.3 collective-permute-start.5
  39.1 0.9 copy.34
  46.9 1.4 fusion.138
  50.7 2.7 %collective-permute-start.11 = (bf16[360,320]{0,1:T(8,128)(2,1)}, bf16[360,320]{0,1:T(8,128)(2,1)}, u32[]{:S(2)}, u32[]{:S(2)}) collective-permute-start(bf16[360,320]{0,1:T(8,128)(2,1)} %collective-permute-done.10), channel_id=1, source_target_pairs={{0,7},{1,0},{2,1},{3,2},{4,3},{5,4},{6,5},{7,6},{8,15},{9,8},{10,9... | collective-permute-start | bytes 691208 | tf_op jit(solution)/shard_map/ppermute | solution.py:69
  53.4 4.9 %collective-permute-done.7 = bf16[360,320]{0,1:T(8,128)(2,1)S(1)} collective-permute-done((bf16[360,320]{0,1:T(8,128)(2,1)}, bf16[360,320]{0,1:T(8,128)(2,1)S(1)}, u32[]{:S(2)}, u32[]{:S(2)}) %collective-permute-start.7) | collective-permute-done | bytes 230432 | tf_op jit(solution)/shard_map/ppermute | solution.py:67
  58.6 2.7 %collective-permute-start.12 = (bf16[360,320]{0,1:T(8,128)(2,1)}, bf16[360,320]{0,1:T(8,128)(2,1)}, u32[]{:S(2)}, u32[]{:S(2)}) collective-permute-start(bf16[360,320]{0,1:T(8,128)(2,1)} %collective-permute-done.11), channel_id=1, source_target_pairs={{0,7},{1,0},{2,1},{3,2},{4,3},{5,4},{6,5},{7,6},{8,15},{9,8},{10,9... | collective-permute-start | bytes 691208 | tf_op jit(solution)/shard_map/ppermute | solution.py:69
  61.3 5.2 %collective-permute-done.8 = bf16[360,320]{0,1:T(8,128)(2,1)} collective-permute-done((bf16[360,320]{0,1:T(8,128)(2,1)S(1)}, bf16[360,320]{0,1:T(8,128)(2,1)}, u32[]{:S(2)}, u32[]{:S(2)}) %collective-permute-start.8) | collective-permute-done | bytes 230432 | tf_op jit(solution)/shard_map/ppermute | solution.py:67
  66.9 2.6 %copy.41 = bf16[8,360,320]{1,2,0:T(8,128)(2,1)} copy(bf16[8,360,320]{2,1,0:T(8,128)(2,1)S(1)} %bitcast.202) | data formatting | bytes 3686400 | tf_op jit(solution)/shard_map/convert_element_type | solution.py:127
  69.8 1.3 copy.26
  73.3 7.5 %concatenate.25 = bf16[5760,320]{0,1:T(8,128)(2,1)} concatenate(bf16[360,320]{0,1:T(8,128)(2,1)} %collective-permute-done.9, bf16[360,320]{0,1:T(8,128)(2,1)} %collective-permute-done.8, bf16[360,320]{0,1:T(8,128)(2,1)} %copy-done.16, bf16[360,320]{0,1:T(8,128)(2,1)} %collective-permute-done.6, bf16[360,320]{0,1:T(8,128)(2,1)} %param.13, ...), dimensions={0} | concatenate | bytes 7372800 | tf_op jit(solution)/shard_map/jit(_roll_dynamic)/concatenate | solution.py:71
  80.9 1.4 fusion.72
  82.3 1.4 fusion.80
  83.6 1.4 fusion.84
  85.0 1.4 fusion.91
  86.4 1.4 fusion.95
  87.8 1.4 fusion.76
  89.1 1.4 fusion.99
  90.5 1.5 fusion.69
  92.1 1.4 fusion.14
  94.5 1.6 fusion.78
  96.0 1.6 fusion.82
  97.6 1.6 fusion.89
  99.2 1.6 fusion.93
  100.8 1.6 fusion.70
  102.4 1.5 fusion.74
  103.9 1.5 fusion.97
  105.5 1.5 fusion.86
  107.0 2.0 %fusion.136 = (f32[320]{0:T(512)S(1)}, f32[320]{0:T(512)S(1)}, f32[384,320]{0,1:T(8,128)S(1)}) fusion(f32[320]{0:T(512)S(1)} %mul.299, f32[320]{0:T(512)S(1)} %sub.62, f32[384,320]{0,1:T(8,128)S(1)} %copy.22, f32[384]{0:T(512)S(1)} %copy-done.27, f32[320]{0:T(512)S(1)} %copy-done.24, f32[320]{0:T(512)S(1)} %copy-done.26, f32[384,320]{0,1:T(8,128)S(1)} %fusion.70, ...), kind=kOutput, calls=%fused_computation.183 | convolution fusion | flops 81960320 | bytes 5415940 | tf_op jit(solution)/shard_map/dot_general | solution.py:113
  109.3 2.8 %collective-permute-start.15 = (f32[32]{0:T(128)S(1)}, f32[32]{0:T(128)S(1)}, u32[]{:S(2)}, u32[]{:S(2)}) collective-permute-start(f32[32]{0:T(128)S(1)} %reduce_sum.72), channel_id=1, source_target_pairs={{0,8},{8,0},{16,24},{24,16},{1,9},{9,1},{17,25},{25,17},{2,10},{10... | collective-permute-start | bytes 392 | tf_op jit(solution)/shard_map/ppermute | solution.py:33
  112.6 1.0 collective-permute-done.15
  113.6 3.0 %collective-permute-start.16 = (f32[32]{0:T(128)S(1)}, f32[32]{0:T(128)S(1)}, u32[]{:S(2)}, u32[]{:S(2)}) collective-permute-start(f32[32]{0:T(128)S(1)} %add.211), channel_id=1, source_target_pairs={{0,16},{8,24},{16,0},{24,8},{1,17},{9,25},{17,1},{25,9},{2,18},{10... | collective-permute-start | bytes 392 | tf_op jit(solution)/shard_map/ppermute | solution.py:33
  116.7 1.8 %collective-permute-start.18 = (f32[32]{0:T(128)S(1)}, f32[32]{0:T(128)S(1)}, u32[]{:S(2)}, u32[]{:S(2)}) collective-permute-start(f32[32]{0:T(128)S(1)} %add.213), channel_id=1, source_target_pairs={{0,16},{8,24},{16,0},{24,8},{1,17},{9,25},{17,1},{25,9},{2,18},{10... | collective-permute-start | bytes 392 | tf_op jit(solution)/shard_map/ppermute | solution.py:33
  118.7 2.4 %collective-permute-done.18 = f32[32]{0:T(128)S(1)} collective-permute-done((f32[32]{0:T(128)S(1)}, f32[32]{0:T(128)S(1)}, u32[]{:S(2)}, u32[]{:S(2)}) %collective-permute-start.18) | collective-permute-done | bytes 160 | tf_op jit(solution)/shard_map/ppermute | solution.py:33
  121.5 1.3 multiply_convert_fusion.1
  122.8 34.1 %all-reduce.4.cloned.1.call-done = bf16[360,320]{0,1:T(8,128)(2,1)} async-done(((bf16[360,320]{0,1:T(8,128)(2,1)}), bf16[360,320]{0,1:T(8,128)(2,1)}) %all-reduce.4.cloned.1.call-update) | async-done | bytes 230416 | tf_op jit(solution)/shard_map/psum | solution.py:133
  156.9 2.2 %fusion.47 = (f32[360,320]{0,1:T(8,128)}, f32[360,320]{0,1:T(8,128)}) fusion(f32[360,320]{0,1:T(8,128)S(1)} %copy-done.17, f32[360,320]{0,1:T(8,128)S(1)} %copy-done.18, bf16[360,320]{0,1:T(8,128)(2,1)} %all-reduce.4.cloned.1.call-done), kind=kLoop, calls=%fused_computation.65 | loop fusion | flops 1382400 | bytes 2073600 | tf_op jit(solution)/shard_map/div | solution.py:143
  (150 shorter events, 20.1 us)
Async XLA Ops:
  7.2 25.4 %copy-start = (bf16[1,3,128,320]{2,3,1,0:T(8,128)(2,1)S(1)}, bf16[1,3,128,320]{2,3,1,0:T(8,128)(2,1)}, u32[]{:S(2)}) copy-start(bf16[1,3,128,320]{2,3,1,0:T(8,128)(2,1)} %param.9) | copy-start | bytes 737284
  7.2 25.4 %copy-start.25 = (f32[320]{0:T(512)S(1)}, f32[320]{0:T(512)}, u32[]{:S(2)}) copy-start(f32[320]{0:T(512)} %param.11) | copy-start | bytes 3844
  7.2 25.4 %copy-start.24 = (f32[320]{0:T(512)S(1)}, f32[320]{0:T(512)}, u32[]{:S(2)}) copy-start(f32[320]{0:T(512)} %param.12) | copy-start | bytes 3844
  7.2 114.3 %reduce-scatter.2.cloned.1.call-start = ((), (), s32[]{:S(2)}) async-start(), calls=%async_computation.1 | async-start | bytes 2211840 | tf_op jit(solution)/shard_map/reduce_scatter | solution.py:126
  7.2 43.0 %collective-permute-start.6 = (bf16[360,320]{0,1:T(8,128)(2,1)}, bf16[360,320]{0,1:T(8,128)(2,1)}, u32[]{:S(2)}, u32[]{:S(2)}) collective-permute-start(bf16[360,320]{0,1:T(8,128)(2,1)} %param.13), channel_id=1, source_target_pairs={{0,1},{1,2},{2,3},{3,4},{4,5},{5,6},{6,7},{7,0},{8,9},{9,10},{10,1... | collective-permute-start | bytes 691208 | tf_op jit(solution)/shard_map/ppermute | solution.py:67
  7.8 42.9 %collective-permute-start.10 = (bf16[360,320]{0,1:T(8,128)(2,1)}, bf16[360,320]{0,1:T(8,128)(2,1)}, u32[]{:S(2)}, u32[]{:S(2)}) collective-permute-start(bf16[360,320]{0,1:T(8,128)(2,1)} %param.13), channel_id=1, source_target_pairs={{0,7},{1,0},{2,1},{3,2},{4,3},{5,4},{6,5},{7,6},{8,15},{9,8},{10,9... | collective-permute-start | bytes 691208 | tf_op jit(solution)/shard_map/ppermute | solution.py:69
  12.1 20.1 %copy-start.28 = (bf16[3,128]{1,0:T(4,128)(2,1)}, bf16[3,128]{1,0:T(4,128)(2,1)S(1)}, u32[]{:S(2)}) copy-start(bf16[3,128]{1,0:T(4,128)(2,1)S(1)} %get-tuple-element.37) | copy-start | bytes 2308
  13.5 11.6 %collective-permute-start = (f32[32]{0:T(128)S(1)}, f32[32]{0:T(128)S(1)}, u32[]{:S(2)}, u32[]{:S(2)}) collective-permute-start(f32[32]{0:T(128)S(1)} %reduce_sum.51), channel_id=1, source_target_pairs={{0,8},{8,0},{16,24},{24,16},{1,9},{9,1},{17,25},{25,17},{2,10},{10... | collective-permute-start | bytes 392 | tf_op jit(solution)/shard_map/ppermute | solution.py:33
  16.0 11.7 %collective-permute-start.2 = (f32[32]{0:T(128)S(1)}, f32[32]{0:T(128)S(1)}, u32[]{:S(2)}, u32[]{:S(2)}) collective-permute-start(f32[32]{0:T(128)S(1)} %reduce_sum.54), channel_id=1, source_target_pairs={{0,8},{8,0},{16,24},{24,16},{1,9},{9,1},{17,25},{25,17},{2,10},{10... | collective-permute-start | bytes 392 | tf_op jit(solution)/shard_map/ppermute | solution.py:33
  17.1 19.1 %collective-permute-start.13 = (bf16[1,128,320]{1,2,0:T(8,128)(2,1)S(1)}, bf16[1,128,320]{1,2,0:T(8,128)(2,1)S(1)}, u32[]{:S(2)}, u32[]{:S(2)}) collective-permute-start(bf16[1,128,320]{1,2,0:T(8,128)(2,1)S(1)} %get-tuple-element.26), channel_id=1, source_target_pairs={{0,8},{8,16},{16,24},{1,9},{9,17},{17,25},{2,10},{10,18},{18,26},{... | collective-permute-start | bytes 245768 | tf_op jit(solution)/shard_map/ppermute | solution.py:17
  25.1 4.5 %collective-permute-start.1 = (f32[32]{0:T(128)S(1)}, f32[32]{0:T(128)S(1)}, u32[]{:S(2)}, u32[]{:S(2)}) collective-permute-start(f32[32]{0:T(128)S(1)} %add.174), channel_id=1, source_target_pairs={{0,16},{8,24},{16,0},{24,8},{1,17},{9,25},{17,1},{25,9},{2,18},{10... | collective-permute-start | bytes 392 | tf_op jit(solution)/shard_map/ppermute | solution.py:33
  27.7 4.4 %collective-permute-start.3 = (f32[32]{0:T(128)S(1)}, f32[32]{0:T(128)S(1)}, u32[]{:S(2)}, u32[]{:S(2)}) collective-permute-start(f32[32]{0:T(128)S(1)} %add.176), channel_id=1, source_target_pairs={{0,16},{8,24},{16,0},{24,8},{1,17},{9,25},{17,1},{25,9},{2,18},{10... | collective-permute-start | bytes 392 | tf_op jit(solution)/shard_map/ppermute | solution.py:33
  29.6 7.9 %collective-permute-start.14 = (bf16[1,128,320]{1,2,0:T(8,128)(2,1)S(1)}, bf16[1,128,320]{1,2,0:T(8,128)(2,1)S(1)}, u32[]{:S(2)}, u32[]{:S(2)}) collective-permute-start(bf16[1,128,320]{1,2,0:T(8,128)(2,1)S(1)} %get-tuple-element.27), channel_id=1, source_target_pairs={{8,0},{16,8},{24,16},{9,1},{17,9},{25,17},{10,2},{18,10},{26,18},{... | collective-permute-start | bytes 245768 | tf_op jit(solution)/shard_map/ppermute | solution.py:19
  32.9 12.5 %collective-permute-start.4 = (bf16[1,128,320]{1,2,0:T(8,128)(2,1)S(1)}, bf16[1,128,320]{1,2,0:T(8,128)(2,1)S(1)}, u32[]{:S(2)}, u32[]{:S(2)}) collective-permute-start(bf16[1,128,320]{1,2,0:T(8,128)(2,1)S(1)} %get-tuple-element.30), channel_id=1, source_target_pairs={{0,8},{8,16},{16,24},{1,9},{9,17},{17,25},{2,10},{10,18},{18,26},{... | collective-permute-start | bytes 245768 | tf_op jit(solution)/shard_map/ppermute | solution.py:17
  36.2 9.3 %collective-permute-start.5 = (bf16[1,128,320]{1,2,0:T(8,128)(2,1)S(1)}, bf16[1,128,320]{1,2,0:T(8,128)(2,1)S(1)}, u32[]{:S(2)}, u32[]{:S(2)}) collective-permute-start(bf16[1,128,320]{1,2,0:T(8,128)(2,1)S(1)} %get-tuple-element.31), channel_id=1, source_target_pairs={{8,0},{16,8},{24,16},{9,1},{17,9},{25,17},{10,2},{18,10},{26,18},{... | collective-permute-start | bytes 245768 | tf_op jit(solution)/shard_map/ppermute | solution.py:19
  45.4 2.8 %copy-start.19 = (bf16[1,128,320]{1,2,0:T(8,128)(2,1)}, bf16[1,128,320]{1,2,0:T(8,128)(2,1)S(1)}, u32[]{:S(2)}) copy-start(bf16[1,128,320]{1,2,0:T(8,128)(2,1)S(1)} %collective-permute-done.4) | copy-start | bytes 245764
  46.8 2.5 %copy-start.10 = (bf16[1,3,128,320]{2,3,1,0:T(8,128)(2,1)S(1)}, bf16[1,3,128,320]{2,3,1,0:T(8,128)(2,1)}, u32[]{:S(2)}) copy-start(bf16[1,3,128,320]{2,3,1,0:T(8,128)(2,1)} %param.10) | copy-start | bytes 737284
  46.8 2.5 %copy-start.29 = (bf16[3,128]{1,0:T(4,128)(2,1)S(1)}, bf16[3,128]{1,0:T(4,128)(2,1)}, u32[]{:S(2)}) copy-start(bf16[3,128]{1,0:T(4,128)(2,1)} %copy-done.28) | copy-start | bytes 2308
  49.3 8.9 %copy-start.22 = (bf16[1,128,320]{1,2,0:T(8,128)(2,1)S(1)}, bf16[1,128,320]{1,2,0:T(8,128)(2,1)}, u32[]{:S(2)}) copy-start(bf16[1,128,320]{1,2,0:T(8,128)(2,1)} %copy-done.21) | copy-start | bytes 245764
  50.3 8.0 %collective-permute-start.7 = (bf16[360,320]{0,1:T(8,128)(2,1)}, bf16[360,320]{0,1:T(8,128)(2,1)S(1)}, u32[]{:S(2)}, u32[]{:S(2)}) collective-permute-start(bf16[360,320]{0,1:T(8,128)(2,1)} %collective-permute-done.6), channel_id=1, source_target_pairs={{0,1},{1,2},{2,3},{3,4},{4,5},{5,6},{6,7},{7,0},{8,9},{9,10},{10,1... | collective-permute-start | bytes 691208 | tf_op jit(solution)/shard_map/ppermute | solution.py:67
  50.7 7.9 %collective-permute-start.11 = (bf16[360,320]{0,1:T(8,128)(2,1)}, bf16[360,320]{0,1:T(8,128)(2,1)}, u32[]{:S(2)}, u32[]{:S(2)}) collective-permute-start(bf16[360,320]{0,1:T(8,128)(2,1)} %collective-permute-done.10), channel_id=1, source_target_pairs={{0,7},{1,0},{2,1},{3,2},{4,3},{5,4},{6,5},{7,6},{8,15},{9,8},{10,9... | collective-permute-start | bytes 691208 | tf_op jit(solution)/shard_map/ppermute | solution.py:69
  58.3 8.6 %copy-start.16 = (bf16[360,320]{0,1:T(8,128)(2,1)}, bf16[360,320]{0,1:T(8,128)(2,1)S(1)}, u32[]{:S(2)}) copy-start(bf16[360,320]{0,1:T(8,128)(2,1)S(1)} %collective-permute-done.7) | copy-start | bytes 691204
  58.3 8.2 %collective-permute-start.8 = (bf16[360,320]{0,1:T(8,128)(2,1)S(1)}, bf16[360,320]{0,1:T(8,128)(2,1)}, u32[]{:S(2)}, u32[]{:S(2)}) collective-permute-start(bf16[360,320]{0,1:T(8,128)(2,1)S(1)} %collective-permute-done.7), channel_id=1, source_target_pairs={{0,1},{1,2},{2,3},{3,4},{4,5},{5,6},{6,7},{7,0},{8,9},{9,10},{10,1... | collective-permute-start | bytes 691208 | tf_op jit(solution)/shard_map/ppermute | solution.py:67
  58.6 14.2 %collective-permute-start.12 = (bf16[360,320]{0,1:T(8,128)(2,1)}, bf16[360,320]{0,1:T(8,128)(2,1)}, u32[]{:S(2)}, u32[]{:S(2)}) collective-permute-start(bf16[360,320]{0,1:T(8,128)(2,1)} %collective-permute-done.11), channel_id=1, source_target_pairs={{0,7},{1,0},{2,1},{3,2},{4,3},{5,4},{6,5},{7,6},{8,15},{9,8},{10,9... | collective-permute-start | bytes 691208 | tf_op jit(solution)/shard_map/ppermute | solution.py:69
  66.5 6.8 %collective-permute-start.9 = (bf16[360,320]{0,1:T(8,128)(2,1)}, bf16[360,320]{0,1:T(8,128)(2,1)}, u32[]{:S(2)}, u32[]{:S(2)}) collective-permute-start(bf16[360,320]{0,1:T(8,128)(2,1)} %collective-permute-done.8), channel_id=1, source_target_pairs={{0,1},{1,2},{2,3},{3,4},{4,5},{5,6},{6,7},{7,0},{8,9},{9,10},{10,1... | collective-permute-start | bytes 691208 | tf_op jit(solution)/shard_map/ppermute | solution.py:67
  69.5 1.9 %copy-start.14 = (bf16[3,128,320]{1,2,0:T(8,128)(2,1)S(1)}, bf16[3,128,320]{1,2,0:T(8,128)(2,1)}, u32[]{:S(2)}) copy-start(bf16[3,128,320]{1,2,0:T(8,128)(2,1)} %get-tuple-element.20) | copy-start | bytes 737284
  69.5 2.1 %copy-start.13 = (bf16[3,128,320]{1,2,0:T(8,128)(2,1)S(1)}, bf16[3,128,320]{1,2,0:T(8,128)(2,1)}, u32[]{:S(2)}) copy-start(bf16[3,128,320]{1,2,0:T(8,128)(2,1)} %get-tuple-element.21) | copy-start | bytes 737284
  69.5 2.3 %copy-start.12 = (bf16[3,128,320]{1,2,0:T(8,128)(2,1)S(1)}, bf16[3,128,320]{1,2,0:T(8,128)(2,1)}, u32[]{:S(2)}) copy-start(bf16[3,128,320]{1,2,0:T(8,128)(2,1)} %get-tuple-element.22) | copy-start | bytes 737284
  69.5 2.6 %copy-start.20 = (bf16[1,128,320]{1,2,0:T(8,128)(2,1)S(1)}, bf16[1,128,320]{1,2,0:T(8,128)(2,1)}, u32[]{:S(2)}) copy-start(bf16[1,128,320]{1,2,0:T(8,128)(2,1)} %copy-done.19) | copy-start | bytes 245764
  69.5 2.6 %copy-start.23 = (bf16[1,128,320]{1,2,0:T(8,128)(2,1)S(1)}, bf16[1,128,320]{1,2,0:T(8,128)(2,1)}, u32[]{:S(2)}) copy-start(bf16[1,128,320]{1,2,0:T(8,128)(2,1)} %copy-done.21) | copy-start | bytes 245764
  69.6 87.3 %all-reduce.4.cloned.1.call-start = ((), (), s32[]{:S(2)}) async-start(), calls=%async_computation.2 | async-start | bytes 491520 | tf_op jit(solution)/shard_map/psum | solution.py:133
  85.0 5.5 %copy-start.26 = (f32[320]{0:T(512)S(1)}, f32[320]{0:T(512)}, u32[]{:S(2)}) copy-start(f32[320]{0:T(512)} %param.11) | copy-start | bytes 3844
  85.0 5.5 %copy-start.30 = (f32[384]{0:T(512)S(1)}, f32[384]{0:T(512)}, u32[]{:S(2)}) copy-start(f32[384]{0:T(512)} %get-tuple-element.36) | copy-start | bytes 4612
  93.5 2.5 %copy-start.6 = (bf16[3,128,320]{2,1,0:T(8,128)(2,1)S(1)}, bf16[3,128,320]{2,1,0:T(8,128)(2,1)}, u32[]{:S(2)}) copy-start(bf16[3,128,320]{2,1,0:T(8,128)(2,1)} %copy.34) | copy-start | bytes 737284
  93.5 4.1 %copy-start.5 = (bf16[3,128,320]{2,1,0:T(8,128)(2,1)S(1)}, bf16[3,128,320]{2,1,0:T(8,128)(2,1)}, u32[]{:S(2)}) copy-start(bf16[3,128,320]{2,1,0:T(8,128)(2,1)} %copy.32) | copy-start | bytes 737284
  93.8 5.5 %copy-start.4 = (bf16[3,128,320]{2,1,0:T(8,128)(2,1)S(1)}, bf16[3,128,320]{2,1,0:T(8,128)(2,1)}, u32[]{:S(2)}) copy-start(bf16[3,128,320]{2,1,0:T(8,128)(2,1)} %copy.31) | copy-start | bytes 737284
  94.0 6.8 %copy-start.3 = (bf16[3,128,320]{2,1,0:T(8,128)(2,1)S(1)}, bf16[3,128,320]{2,1,0:T(8,128)(2,1)}, u32[]{:S(2)}) copy-start(bf16[3,128,320]{2,1,0:T(8,128)(2,1)} %copy.37) | copy-start | bytes 737284
  96.0 6.4 %copy-start.8 = (bf16[3,128,320]{2,1,0:T(8,128)(2,1)S(1)}, bf16[3,128,320]{2,1,0:T(8,128)(2,1)}, u32[]{:S(2)}) copy-start(bf16[3,128,320]{2,1,0:T(8,128)(2,1)} %copy.36) | copy-start | bytes 737284
  97.6 6.3 %copy-start.9 = (bf16[3,128,320]{2,1,0:T(8,128)(2,1)S(1)}, bf16[3,128,320]{2,1,0:T(8,128)(2,1)}, u32[]{:S(2)}) copy-start(bf16[3,128,320]{2,1,0:T(8,128)(2,1)} %copy.30) | copy-start | bytes 737284
  99.2 6.3 %copy-start.2 = (bf16[384,320]{1,0:T(8,128)(2,1)S(1)}, bf16[384,320]{1,0:T(8,128)(2,1)}, u32[]{:S(2)}) copy-start(bf16[384,320]{1,0:T(8,128)(2,1)} %bitcast_multiply_fusion.1) | copy-start | bytes 737284
  100.8 6.2 %copy-start.1 = (bf16[3,128,320]{2,1,0:T(8,128)(2,1)S(1)}, bf16[3,128,320]{2,1,0:T(8,128)(2,1)}, u32[]{:S(2)}) copy-start(bf16[3,128,320]{2,1,0:T(8,128)(2,1)} %copy.29) | copy-start | bytes 737284
  100.8 6.2 %copy-start.27 = (f32[384]{0:T(512)S(1)}, f32[384]{0:T(512)}, u32[]{:S(2)}) copy-start(f32[384]{0:T(512)} %get-tuple-element.34) | copy-start | bytes 4612
  109.0 47.8 %copy-start.17 = (f32[360,320]{0,1:T(8,128)S(1)}, f32[360,320]{0,1:T(8,128)}, u32[]{:S(2)}) copy-start(f32[360,320]{0,1:T(8,128)} %param.15) | copy-start | bytes 1382404
  109.1 47.8 %copy-start.18 = (f32[360,320]{0,1:T(8,128)S(1)}, f32[360,320]{0,1:T(8,128)}, u32[]{:S(2)}) copy-start(f32[360,320]{0,1:T(8,128)} %param.14) | copy-start | bytes 1382404
  109.3 4.3 %collective-permute-start.15 = (f32[32]{0:T(128)S(1)}, f32[32]{0:T(128)S(1)}, u32[]{:S(2)}, u32[]{:S(2)}) collective-permute-start(f32[32]{0:T(128)S(1)} %reduce_sum.72), channel_id=1, source_target_pairs={{0,8},{8,0},{16,24},{24,16},{1,9},{9,1},{17,25},{25,17},{2,10},{10... | collective-permute-start | bytes 392 | tf_op jit(solution)/shard_map/ppermute | solution.py:33
  112.3 4.3 %collective-permute-start.17 = (f32[32]{0:T(128)S(1)}, f32[32]{0:T(128)S(1)}, u32[]{:S(2)}, u32[]{:S(2)}) collective-permute-start(f32[32]{0:T(128)S(1)} %reduce_sum.75), channel_id=1, source_target_pairs={{0,8},{8,0},{16,24},{24,16},{1,9},{9,1},{17,25},{25,17},{2,10},{10... | collective-permute-start | bytes 392 | tf_op jit(solution)/shard_map/ppermute | solution.py:33
  113.6 5.1 %collective-permute-start.16 = (f32[32]{0:T(128)S(1)}, f32[32]{0:T(128)S(1)}, u32[]{:S(2)}, u32[]{:S(2)}) collective-permute-start(f32[32]{0:T(128)S(1)} %add.211), channel_id=1, source_target_pairs={{0,16},{8,24},{16,0},{24,8},{1,17},{9,25},{17,1},{25,9},{2,18},{10... | collective-permute-start | bytes 392 | tf_op jit(solution)/shard_map/ppermute | solution.py:33
  116.7 4.4 %collective-permute-start.18 = (f32[32]{0:T(128)S(1)}, f32[32]{0:T(128)S(1)}, u32[]{:S(2)}, u32[]{:S(2)}) collective-permute-start(f32[32]{0:T(128)S(1)} %add.213), channel_id=1, source_target_pairs={{0,16},{8,24},{16,0},{24,8},{1,17},{9,25},{17,1},{25,9},{2,18},{10... | collective-permute-start | bytes 392 | tf_op jit(solution)/shard_map/ppermute | solution.py:33
  (4 other events, 4.7 us)
Sparse Core Ops, SparseCore 0:
  69.7 44.7 reduce-scatter.1
  121.6 35.1 all-reduce.3
